TPU v7x, 32 devices: a whole 2x2x4 slice. The times are simulated.
32 devices in a mesh: groups: 2 (over y), tensor: 4 (over z), seq: 2 (over x), load: 2 (over core).
Axes of the slice: x: 2, y: 2, z: 4, core: 2. Of those that a mesh axis runs over, the one named last changes fastest.
Arguments:
- tokens: bfloat16 [1024, 16384], P(('groups', 'tensor'), ('seq', 'load')), parts along dimension 0, may hold values from -21 to 21
- weight_query: bfloat16 [16384, 16384], P(('seq', 'load'), 'tensor'), may hold values from -0.046875 to 0.046875
- weight_keyval: bfloat16 [16384, 2048], P(('seq', 'load'), 'tensor'), may hold values from -0.046875 to 0.046875
- down_query: bfloat16 [16384, 1024], P(('seq', 'load'), ('groups', 'tensor')), parts along dimension 1, may hold values from -0.046875 to 0.046875
- down_keyval: bfloat16 [16384, 1024], P(('seq', 'load'), ('groups', 'tensor')), parts along dimension 1, may hold values from -0.046875 to 0.046875
- up_query: bfloat16 [1024, 16384], P(('groups', 'load'), 'tensor'), parts along dimension 0, may hold values from -0.5 to 0.5
- up_keyval: bfloat16 [1024, 2048], P(('groups', 'load'), 'tensor'), parts along dimension 0, may hold values from -0.5 to 0.5
- adapter_rank: int32 [8], P('groups'), parts along dimension 0, may hold values from 8 to 128, as said below
- token_lengths: int32 [8], P('groups'), parts along dimension 0, may hold values from 1 to 384, 512 in all
- adapter_slot: int32 [8], P('groups'), parts along dimension 0, may hold values from 0 to 3, each once
Outputs:
- context: bfloat16 [1024, 16384], P(('groups', 'seq', 'load'), 'tensor'), parts along dimension 0
- kv_cache: bfloat16 [1024, 2048], P(('groups', 'seq', 'load'), 'tensor'), parts along dimension 0
There are 2 independent parts, one for each index of `groups`. A program takes and returns all parts, laid end to end along the dimension named above; an argument that names none is the same for every part. Nothing has to cross between parts.
Inputs may be any that keep to these rules, and one draw needn't show every extreme that they name: `adapter_rank`: each rank is a power of two; some tenant has rank 128 and some has rank 8. `token_lengths`: the lengths sum to 512; some tenant has exactly 384 tokens. `adapter_slot`: each slot belongs to exactly one tenant.
All inputs are finite; a program needn't handle non-finite values.
Results may differ from a plain program's by a relative error of at most 0.0025.
The roundings to bfloat16 on the way count: a program that leaves them out, or rounds other values in their place, can miss the bound.
Values may be sent and summed in bfloat16 or wider, within the bound.
No kernel may reach another device: no remote copies, remote signals or barrier semaphores. Data moves between devices by JAX's collectives and lax.ppermute only.
A program may use at most 128 MiB of HBM per device.

v0:
```python
import math
import jax
import jax.numpy as jnp
from jax import lax
from jax.sharding import PartitionSpec as P

HEADS = 128
KV_HEADS = 8
HEAD_DIM = 128
TENANTS = 4
ROPE_BASE = 500000.0
ADAPTER_ALPHA = 8.0


def product(left, right):
    return jnp.dot(left, right, preferred_element_type=jnp.float32)


def rotate_pairs(values, position, first_col):
    pair_count = values.shape[1] // 2
    pair_col = first_col + 2 * jnp.arange(pair_count, dtype=jnp.int32)
    within = pair_col % HEAD_DIM // 2
    frequency = jnp.exp(-(2.0 * within.astype(jnp.float32) / HEAD_DIM) * math.log(ROPE_BASE))
    angles = position.astype(jnp.float32)[:, None] * frequency[None, :]
    pair_view = values.reshape(values.shape[0], pair_count, 2)
    even_part = pair_view[:, :, 0]
    odd_part = pair_view[:, :, 1]
    cosine = jnp.cos(angles)
    sine_angle = jnp.sin(angles)
    turned = jnp.stack(
        [even_part * cosine - odd_part * sine_angle, even_part * sine_angle + odd_part * cosine],
        axis=2,
    )
    return turned.reshape(values.shape)


def tenant_table(token_ids, adapter_rank, token_lengths, adapter_slot):
    segment_ends = jnp.cumsum(token_lengths)
    begins = segment_ends - token_lengths
    owned_rows = (token_ids[:, None] >= begins[None, :]) & (
        token_ids[:, None] < segment_ends[None, :]
    )
    zero_int = jnp.zeros((), jnp.int32)
    own_rank = jnp.sum(jnp.where(owned_rows, adapter_rank[None, :], zero_int), axis=1)
    own_slot = jnp.sum(jnp.where(owned_rows, adapter_slot[None, :], zero_int), axis=1)
    own_first = jnp.sum(jnp.where(owned_rows, begins[None, :], zero_int), axis=1)
    slot_hot = own_slot[:, None] == jnp.arange(TENANTS, dtype=jnp.int32)[None, :]
    return (own_rank, own_first, slot_hot)


def select_slot(down_values, slot_hot):
    shaped = down_values.reshape(down_values.shape[0], -1, TENANTS)
    return jnp.sum(jnp.where(slot_hot[:, None, :], shaped, 0.0), axis=2)


def scale_ranks(picked, own_rank, first_rank):
    rank_index = first_rank + jnp.arange(picked.shape[1], dtype=jnp.int32)
    keep_mask = rank_index[None, :] < own_rank[:, None]
    factor = ADAPTER_ALPHA / jnp.sqrt(own_rank.astype(jnp.float32))
    return jnp.where(keep_mask, picked * factor[:, None], 0.0).astype(jnp.bfloat16)


def widen_slots(low_values, slot_hot):
    wide_rows = jnp.where(
        slot_hot[:, None, :], low_values[:, :, None], jnp.zeros((), low_values.dtype)
    )
    return wide_rows.reshape(low_values.shape[0], -1)


def shards(
    tokens,
    weight_query,
    weight_keyval,
    down_query,
    down_keyval,
    up_query,
    up_keyval,
    adapter_rank,
    token_lengths,
    adapter_slot,
):
    tensor_count = lax.axis_size("tensor")
    block_count = lax.axis_size(("seq", "load"))
    tensor_index = lax.axis_index("tensor")
    block_index = lax.axis_index(("seq", "load"))
    query_cols = weight_query.shape[1]
    keyval_cols = weight_keyval.shape[1]
    rank_share = down_query.shape[1] // TENANTS
    block_rows = tokens.shape[0] * tensor_count // block_count
    shard_rows = lax.all_gather(tokens, "tensor", axis=0, tiled=True)
    piece_ids = jnp.arange(shard_rows.shape[0], dtype=jnp.int32)
    piece_rank, piece_first, piece_hot = tenant_table(
        piece_ids, adapter_rank, token_lengths, adapter_slot
    )
    columns_list = [
        product(shard_rows, weight_query),
        product(shard_rows, weight_keyval),
        select_slot(product(shard_rows, down_query), piece_hot),
        select_slot(product(shard_rows, down_keyval), piece_hot),
    ]
    partial_terms = jnp.concatenate(columns_list, axis=1)
    summed = lax.psum_scatter(partial_terms, ("seq", "load"), scatter_dimension=0, tiled=True)
    token_ids = block_index * block_rows + jnp.arange(block_rows, dtype=jnp.int32)
    own_rank, own_first, slot_hot = tenant_table(
        token_ids, adapter_rank, token_lengths, adapter_slot
    )
    position = token_ids - own_first
    low_start = query_cols + keyval_cols
    first_rank = tensor_index * rank_share
    low_query = scale_ranks(summed[:, low_start : low_start + rank_share], own_rank, first_rank)
    low_keyval = scale_ranks(summed[:, low_start + rank_share :], own_rank, first_rank)
    full_query, full_keyval = (
        lax.all_gather(low_query, "tensor", axis=1, tiled=True),
        lax.all_gather(low_keyval, "tensor", axis=1, tiled=True),
    )
    wide_query = widen_slots(full_query, slot_hot)
    wide_keyval = widen_slots(full_keyval, slot_hot)
    up_query_all, up_keyval_all = (
        lax.all_gather(up_query, "load", axis=0, tiled=True),
        lax.all_gather(up_keyval, "load", axis=0, tiled=True),
    )
    delta_query = product(wide_query, up_query_all)
    delta_keyval = product(wide_keyval, up_keyval_all)
    query_rows = rotate_pairs(
        summed[:, :query_cols] + delta_query, position, tensor_index * query_cols
    ).astype(jnp.bfloat16)
    keyval = summed[:, query_cols:low_start] + delta_keyval
    kv_first_col = tensor_index * keyval_cols
    is_key = kv_first_col + jnp.arange(keyval_cols, dtype=jnp.int32) < KV_HEADS * HEAD_DIM
    kv_local = jnp.where(
        is_key[None, :], rotate_pairs(keyval, position, kv_first_col), keyval
    ).astype(jnp.bfloat16)
    kv_all = lax.all_gather(kv_local, "tensor", axis=1, tiled=True)
    heads_here = query_cols // HEAD_DIM
    group_size = HEADS // KV_HEADS
    kv_here = max(heads_here // group_size, 1)
    per_kv = heads_here // kv_here
    kv_first = tensor_index * heads_here // group_size
    key_cols = KV_HEADS * HEAD_DIM
    key_heads = lax.dynamic_slice_in_dim(
        kv_all, kv_first * HEAD_DIM, kv_here * HEAD_DIM, 1
    ).reshape(block_rows, kv_here, HEAD_DIM)
    value_heads = lax.dynamic_slice_in_dim(
        kv_all, key_cols + kv_first * HEAD_DIM, kv_here * HEAD_DIM, 1
    ).reshape(block_rows, kv_here, HEAD_DIM)
    grouped = query_rows.reshape(block_rows, kv_here, per_kv, HEAD_DIM)
    running_top = jnp.full((kv_here, per_kv, block_rows), -1e30, jnp.float32)
    piece_keys = lax.all_gather(key_heads, ("seq", "load"), axis=0, tiled=True)
    piece_values = lax.all_gather(value_heads, ("seq", "load"), axis=0, tiled=True)
    key_ids = jnp.arange(piece_keys.shape[0], dtype=jnp.int32)
    visible = (key_ids[None, :] >= own_first[:, None]) & (key_ids[None, :] <= token_ids[:, None])
    scores = jnp.einsum(
        "qghd,kgd->ghqk", grouped, piece_keys, preferred_element_type=jnp.float32
    ) / math.sqrt(HEAD_DIM)
    scores = jnp.where(visible, scores, -1e30)
    new_top = jnp.maximum(running_top, jnp.max(scores, axis=3))
    exp_scores = jnp.where(visible, jnp.exp(scores - new_top[..., None]), 0.0)
    new_sum = jnp.sum(exp_scores, axis=3)
    new_acc = jnp.einsum(
        "ghqk,kgd->ghqd",
        exp_scores.astype(jnp.bfloat16),
        piece_values,
        preferred_element_type=jnp.float32,
    )
    state_tuple = (new_top, new_sum, new_acc)
    final_top, row_total, accumulated = state_tuple
    context = (accumulated / row_total[..., None]).astype(jnp.bfloat16)
    context = jnp.transpose(context, (2, 0, 1, 3)).reshape(block_rows, query_cols)
    return (context, kv_local)


def solution(mesh):
    placed = (
        P(("groups", "tensor"), ("seq", "load")),
        P(("seq", "load"), "tensor"),
        P(("seq", "load"), "tensor"),
        P(("seq", "load"), ("groups", "tensor")),
        P(("seq", "load"), ("groups", "tensor")),
        P(("groups", "load"), "tensor"),
        P(("groups", "load"), "tensor"),
        P("groups"),
        P("groups"),
        P("groups"),
    )
    return jax.shard_map(
        shards,
        mesh=mesh,
        in_specs=placed,
        out_specs=(P(("groups", "seq", "load"), "tensor"), P(("groups", "seq", "load"), "tensor")),
        check_vma=False,
    )
```

profile of v0, /device:TPU:0, one launch (start us, length us, event | category | flops | bytes accessed | tf_op | source)
XLA Modules:
  0.0 307.8 jit_solution(12603682997678167109)
XLA Ops:
  8.8 0.8 reduce-window.8
  11.0 82.9 %all-gather.3.cloned.1.call-done = bf16[512,4096]{1,0:T(8,128)(2,1)} async-done(((bf16[128,4096]{1,0:T(8,128)(2,1)}), bf16[512,4096]{1,0:T(8,128)(2,1)}) %all-gather.3.cloned.1.call-update) | async-done | bytes 4194320 | tf_op jit(solution)/shard_map/all_gather | solution.py:90
  93.9 3.7 %fusion.46 = f32[512,128]{0,1:T(8,128)S(1)} fusion(bf16[512,4096]{1,0:T(8,128)(2,1)} %all-gather.3.cloned.1.call-done, bf16[4096,128]{1,0:T(8,128)(2,1)S(1)} %copy-done), kind=kOutput, calls=%fused_computation.100 | convolution fusion | flops 536870912 | bytes 5505024 | tf_op jit(solution)/shard_map/dot_general | solution.py:16
  97.7 3.7 %fusion.47 = f32[512,128]{0,1:T(8,128)S(1)} fusion(bf16[512,4096]{1,0:T(8,128)(2,1)} %all-gather.3.cloned.1.call-done, bf16[4096,128]{1,0:T(8,128)(2,1)S(1)} %copy-done.4), kind=kOutput, calls=%fused_computation.101 | convolution fusion | flops 536870912 | bytes 5505024 | tf_op jit(solution)/shard_map/dot_general | solution.py:16
  101.9 26.5 %fusion.44 = f32[512,4096]{0,1:T(8,128)} fusion(bf16[512,4096]{1,0:T(8,128)(2,1)} %all-gather.3.cloned.1.call-done, bf16[4096,4096]{1,0:T(8,128)(2,1)} %param.11), kind=kOutput, calls=%fused_computation.98 | convolution fusion | flops 17179869184 | bytes 46137344 | tf_op jit(solution)/shard_map/dot_general | solution.py:16
  128.4 4.7 %fusion.45 = f32[512,512]{0,1:T(8,128)S(1)} fusion(bf16[512,4096]{1,0:T(8,128)(2,1)S(1)} %copy-done.2, bf16[4096,512]{1,0:T(8,128)(2,1)} %param.12), kind=kOutput, calls=%fused_computation.99 | convolution fusion | flops 2147483648 | bytes 9437184 | tf_op jit(solution)/shard_map/dot_general | solution.py:16
  133.1 9.8 %pad_maximum_fusion = f32[512,4672]{0,1:T(8,128)} fusion(f32[512,32]{0,1:T(8,128)S(1)} %get-tuple-element.13, f32[512,32]{0,1:T(8,128)S(1)} %get-tuple-element.12, f32[512,512]{0,1:T(8,128)S(1)} %fusion.45, f32[512,4096]{0,1:T(8,128)S(1)} %copy-done.3), kind=kLoop, calls=%fused_computation | loop fusion | flops 7176192 | bytes 19136512 | tf_op jit(solution)/shard_map/concatenate | solution.py:101
  143.8 2.2 all_gather.26
  146.1 76.7 %reduce-scatter.2.cloned.1.call-done = f32[128,4672]{0,1:T(8,128)} async-done(((f32[512,4672]{0,1:T(8,128)}), f32[128,4672]{0,1:T(8,128)}) %reduce-scatter.2.cloned.1.call-update) | async-done | bytes 2392080 | tf_op jit(solution)/shard_map/reduce_scatter | solution.py:102
  222.8 0.8 fusion.27
  223.7 13.2 %all_gather.25 = bf16[128,128]{0,1:T(8,128)(2,1)S(1)} all-gather(bf16[128,32]{0,1:T(8,128)(2,1)S(1)} %get-tuple-element.17), channel_id=1, replica_groups=mesh['groups'=2,'tensor'=4,'seq'=2,'load'=2] {'tensor'}, dimensions={1}, use_global_device_ids=true | all-gather | bytes 40960 | tf_op jit(solution)/shard_map/all_gather | solution.py:114
  236.8 13.1 %all_gather.29 = bf16[128,128]{0,1:T(8,128)(2,1)S(1)} all-gather(bf16[128,32]{0,1:T(8,128)(2,1)S(1)} %get-tuple-element.18), channel_id=1, replica_groups=mesh['groups'=2,'tensor'=4,'seq'=2,'load'=2] {'tensor'}, dimensions={1}, use_global_device_ids=true | all-gather | bytes 40960 | tf_op jit(solution)/shard_map/all_gather | solution.py:113
  250.1 1.3 convolution_add_fusion.1
  253.4 15.4 %all_gather.27 = bf16[128,2048]{0,1:T(8,128)(2,1)S(1)} all-gather(bf16[128,512]{0,1:T(8,128)(2,1)S(1)} %select_convert_fusion), channel_id=1, replica_groups=mesh['groups'=2,'tensor'=4,'seq'=2,'load'=2] {'tensor'}, dimensions={1}, use_global_device_ids=true | all-gather | bytes 655360 | tf_op jit(solution)/shard_map/all_gather | solution.py:133
  269.0 5.8 %all_gather.28 = bf16[512,2,128]{2,0,1:T(8,128)(2,1)S(1)} all-gather(bf16[128,2,128]{2,0,1:T(8,128)(2,1)S(1)} %copy.60), channel_id=1, replica_groups=mesh['groups'=2,'tensor'=4,'seq'=2,'load'=2] {'seq','load'}, dimensions={0}, use_global_device_ids=true | all-gather | bytes 327680 | tf_op jit(solution)/shard_map/all_gather | solution.py:148
  274.8 4.6 %convolution_add_fusion = f32[128,4096]{0,1:T(8,128)S(1)} fusion(bf16[128,512]{0,1:T(8,128)(2,1)S(1)} %bitcast.63, bf16[512,4096]{1,0:T(8,128)(2,1)} %all-gather.5.cloned.1.call-done, f32[128,4672]{0,1:T(8,128)} %reduce-scatter.2.cloned.1.call-done), kind=kOutput, calls=%fused_computation.6 | convolution fusion | flops 537395200 | bytes 8519680 | tf_op jit(solution)/shard_map/dot_general | solution.py:16
  279.4 1.7 fusion.42
  282.4 4.2 %fusion.14 = (bf16[128,2048,1]{1,0,2:T(8,128)(2,1)S(1)}, bf16[128,2048,1]{1,0,2:T(8,128)(2,1)S(1)}) fusion(f32[128,2048,1]{1,0,2:T(8,128)S(1)} %copy.79, f32[128,2048,1]{1,0,2:T(8,128)S(1)} %copy.78, f32[2048]{0:T(1024)S(1)} %fusion.35, f32[128]{0:T(128)S(1)} %subtract_convert_fusion), kind=kLoop, calls=%fused_computation.19 | loop fusion | flops 2359296 | bytes 3154432 | tf_op jit(solution)/shard_map/convert
  286.7 0.8 copy.64
  287.5 1.3 fusion
  288.8 5.9 %all_gather.31 = bf16[512,2,128]{0,2,1:T(8,128)(2,1)S(1)} all-gather(bf16[128,2,128]{0,2,1:T(8,128)(2,1)S(1)} %bitcast.66), channel_id=1, replica_groups=mesh['groups'=2,'tensor'=4,'seq'=2,'load'=2] {'seq','load'}, dimensions={0}, use_global_device_ids=true | all-gather | bytes 327680 | tf_op jit(solution)/shard_map/all_gather | solution.py:149
  294.7 2.0 fusion.1
  296.8 2.2 fusion.6
  299.0 1.3 copy.67
  (54 shorter events, 7.4 us)
Async XLA Ops:
  8.0 85.9 %copy-start = (bf16[4096,128]{1,0:T(8,128)(2,1)S(1)}, bf16[4096,128]{1,0:T(8,128)(2,1)}, u32[]{:S(2)}) copy-start(bf16[4096,128]{1,0:T(8,128)(2,1)} %param.13) | copy-start | bytes 3145732
  8.0 89.7 %copy-start.4 = (bf16[4096,128]{1,0:T(8,128)(2,1)S(1)}, bf16[4096,128]{1,0:T(8,128)(2,1)}, u32[]{:S(2)}) copy-start(bf16[4096,128]{1,0:T(8,128)(2,1)} %param.14) | copy-start | bytes 3145732
  8.0 85.9 %all-gather.3.cloned.1.call-start = ((), (), s32[]{:S(2)}) async-start(), calls=%async_computation.1 | async-start | bytes 5242880 | tf_op jit(solution)/shard_map/all_gather | solution.py:90
  8.8 214.1 %reduce-scatter.2.cloned.1.call-start = ((), (), s32[]{:S(2)}) async-start(), calls=%async_computation.2 | async-start | bytes 11960320 | tf_op jit(solution)/shard_map/reduce_scatter | solution.py:102
  101.9 26.5 %copy-start.2 = (bf16[512,4096]{1,0:T(8,128)(2,1)S(1)}, bf16[512,4096]{1,0:T(8,128)(2,1)}, u32[]{:S(2)}) copy-start(bf16[512,4096]{1,0:T(8,128)(2,1)} %all-gather.3.cloned.1.call-done) | copy-start | bytes 12582916
  128.4 4.7 %copy-start.3 = (f32[512,4096]{0,1:T(8,128)S(1)}, f32[512,4096]{0,1:T(8,128)}, u32[]{:S(2)}) copy-start(f32[512,4096]{0,1:T(8,128)} %fusion.44) | copy-start | bytes 25165828
  142.9 0.7 copy-start.6
  142.9 0.7 copy-start.7
  142.9 1.0 copy-start.5
  142.9 131.9 %all-gather.5.cloned.1.call-start = ((), (), s32[]{:S(2)}) async-start(), calls=%async_computation.3 | async-start | bytes 6291456 | tf_op jit(solution)/shard_map/all_gather | solution.py:119
  296.8 3.5 %copy-start.1 = (bf16[4096,128]{1,0:T(8,128)(2,1)S(1)}, bf16[4096,128]{1,0:T(8,128)(2,1)}, u32[]{:S(2)}) copy-start(bf16[4096,128]{1,0:T(8,128)(2,1)} %param.13) | copy-start | bytes 3145732
Sparse Core Ops, SparseCore 0:
  10.4 83.4 all-gather.2
  143.0 79.7 reduce-scatter.1
Sparse Core Ops, SparseCore 1:
  144.9 12.6 all-gather.4
where the time goes:
time: 308 us
  waiting for transfers between devices  161 us (52%)
  blocking collectives  55.6 us (18%)
  matrix products  48 us (16%)
  other arithmetic  20.6 us (7%)
  between operations  15.8 us (5%)
  local copies, waits for them, and re-layouts  6.82 us (2%)
    all_gather x1, waiting for transfers between devices, shards(): shard_rows = lax.all_gather(tokens, 'tensor', axis=0, tiled=True)  82.9 us
    reduce_scatter x1, waiting for transfers between devices, shards(): lax.psum_scatter(partial_terms, ('seq', 'load'), scatter_dimension=0, til...  76.7 us
    dot_general x6, matrix products, product(): return jnp.dot(left, right, preferred_element_type=jnp.float32)  44.5 us
    all_gather x1, blocking collectives, shards(): kv_all = lax.all_gather(kv_local, 'tensor', axis=1, tiled=True)  15.4 us
    all_gather x1, blocking collectives, shards(): lax.all_gather(low_keyval, 'tensor', axis=1, tiled=True)  13.2 us
    all_gather x1, blocking collectives, shards(): lax.all_gather(low_query, 'tensor', axis=1, tiled=True)  13.1 us
    concatenate x1, other arithmetic, shards(): partial_terms = jnp.concatenate(columns_list, axis=1)  9.75 us
  transfers between devices with their start and end apart: 3, of which 2 were waited for; matrix products, arithmetic and copies ran while one was open for 2% of the time, Pallas kernels for 0%

commit v1 on v0

--- a/solution.py
+++ b/solution.py
@@ -130,7 +130,14 @@
     kv_local = jnp.where(
         is_key[None, :], rotate_pairs(keyval, position, kv_first_col), keyval
     ).astype(jnp.bfloat16)
-    kv_all = lax.all_gather(kv_local, "tensor", axis=1, tiled=True)
+    ring = [kv_local]
+    for hop in range(3):
+        ring.append(lax.ppermute(ring[-1], "tensor", [(dev, (dev + 1) % 4) for dev in range(4)]))
+    kv_all = jnp.roll(
+        jnp.concatenate(ring[::-1], axis=1),
+        (lax.axis_index("tensor") + 1) * ring[0].shape[1],
+        axis=1,
+    )
     heads_here = query_cols // HEAD_DIM
     group_size = HEADS // KV_HEADS
     kv_here = max(heads_here // group_size, 1)

time: 308 us -> 305 us (level)
  blocking collectives: 55.6 us -> 40.2 us
  waiting for transfers between devices: 161 us -> 166 us
  starting transfers between devices: 0.12 us -> 3.36 us
    all_gather x1 -> x0, blocking collectives: 15.4 us -> none  [shards(): kv_all = lax.all_gather(kv_local, 'tensor', axis=1, tiled=True)]
    ppermute x0 -> x3, waiting for transfers between devices: none -> 5.11 us  [shards(): lax.ppermute(ring[-1], 'tensor', [(dev, (dev + 1) % 4) for dev in range(4)])]
    ppermute x0 -> x3, starting transfers between devices: none -> 3.24 us  [shards(): lax.ppermute(ring[-1], 'tensor', [(dev, (dev + 1) % 4) for dev in range(4)])]
  transfers between devices with their start and end apart: 3 -> 6, of which waited for: 2 -> 4; matrix products, arithmetic and copies ran while one was open for 2% -> 7% of each run, Pallas kernels for 0% -> 0%
where the time goes in v1:
time: 305 us
  waiting for transfers between devices  166 us (54%)
  matrix products  48 us (16%)
  blocking collectives  40.2 us (13%)
  other arithmetic  22.5 us (7%)
  between operations  15.9 us (5%)
  local copies, waits for them, and re-layouts  8.79 us (3%)
  starting transfers between devices  3.36 us (1%)
    all_gather x1, waiting for transfers between devices, shards(): shard_rows = lax.all_gather(tokens, 'tensor', axis=0, tiled=True)  82.9 us
    reduce_scatter x1, waiting for transfers between devices, shards(): lax.psum_scatter(partial_terms, ('seq', 'load'), scatter_dimension=0, til...  76.7 us
    dot_general x6, matrix products, product(): return jnp.dot(left, right, preferred_element_type=jnp.float32)  44.5 us
    all_gather x1, blocking collectives, shards(): lax.all_gather(low_keyval, 'tensor', axis=1, tiled=True)  13.2 us
    all_gather x1, blocking collectives, shards(): lax.all_gather(low_query, 'tensor', axis=1, tiled=True)  13.1 us
    concatenate x1, other arithmetic, shards(): partial_terms = jnp.concatenate(columns_list, axis=1)  9.76 us
  transfers between devices with their start and end apart: 6, of which 4 were waited for; matrix products, arithmetic and copies ran while one was open for 7% of the time, Pallas kernels for 0%

profile of v1, /device:TPU:0, one launch (start us, length us, event | category | flops | bytes accessed | tf_op | source)
XLA Modules:
  0.0 304.7 jit_solution(8174041308665925283)
XLA Ops:
  11.0 82.9 %all-gather.3.cloned.1.call-done = bf16[512,4096]{1,0:T(8,128)(2,1)} async-done(((bf16[128,4096]{1,0:T(8,128)(2,1)}), bf16[512,4096]{1,0:T(8,128)(2,1)}) %all-gather.3.cloned.1.call-update) | async-done | bytes 4194320 | tf_op jit(solution)/shard_map/all_gather | solution.py:90
  93.9 3.7 %fusion.46 = f32[512,128]{0,1:T(8,128)S(1)} fusion(bf16[512,4096]{1,0:T(8,128)(2,1)} %all-gather.3.cloned.1.call-done, bf16[4096,128]{1,0:T(8,128)(2,1)S(1)} %copy-done), kind=kOutput, calls=%fused_computation.108 | convolution fusion | flops 536870912 | bytes 5505024 | tf_op jit(solution)/shard_map/dot_general | solution.py:16
  97.7 3.7 %fusion.47 = f32[512,128]{0,1:T(8,128)S(1)} fusion(bf16[512,4096]{1,0:T(8,128)(2,1)} %all-gather.3.cloned.1.call-done, bf16[4096,128]{1,0:T(8,128)(2,1)S(1)} %copy-done.4), kind=kOutput, calls=%fused_computation.109 | convolution fusion | flops 536870912 | bytes 5505024 | tf_op jit(solution)/shard_map/dot_general | solution.py:16
  101.9 26.5 %fusion.44 = f32[512,4096]{0,1:T(8,128)} fusion(bf16[512,4096]{1,0:T(8,128)(2,1)} %all-gather.3.cloned.1.call-done, bf16[4096,4096]{1,0:T(8,128)(2,1)} %param.11), kind=kOutput, calls=%fused_computation.106 | convolution fusion | flops 17179869184 | bytes 46137344 | tf_op jit(solution)/shard_map/dot_general | solution.py:16
  128.4 4.7 %fusion.45 = f32[512,512]{0,1:T(8,128)S(1)} fusion(bf16[512,4096]{1,0:T(8,128)(2,1)S(1)} %copy-done.2, bf16[4096,512]{1,0:T(8,128)(2,1)} %param.12), kind=kOutput, calls=%fused_computation.107 | convolution fusion | flops 2147483648 | bytes 9437184 | tf_op jit(solution)/shard_map/dot_general | solution.py:16
  133.1 9.8 %pad_maximum_fusion = f32[512,4672]{0,1:T(8,128)} fusion(f32[512,32]{0,1:T(8,128)S(1)} %get-tuple-element.13, f32[512,32]{0,1:T(8,128)S(1)} %get-tuple-element.12, f32[512,512]{0,1:T(8,128)S(1)} %fusion.45, f32[512,4096]{0,1:T(8,128)S(1)} %copy-done.3), kind=kLoop, calls=%fused_computation | loop fusion | flops 7176192 | bytes 19136512 | tf_op jit(solution)/shard_map/concatenate | solution.py:101
  143.9 2.2 all_gather.23
  146.1 76.7 %reduce-scatter.2.cloned.1.call-done = f32[128,4672]{0,1:T(8,128)} async-done(((f32[512,4672]{0,1:T(8,128)}), f32[128,4672]{0,1:T(8,128)}) %reduce-scatter.2.cloned.1.call-update) | async-done | bytes 2392080 | tf_op jit(solution)/shard_map/reduce_scatter | solution.py:102
  223.7 13.2 %all_gather.22 = bf16[128,128]{0,1:T(8,128)(2,1)S(1)} all-gather(bf16[128,32]{0,1:T(8,128)(2,1)S(1)} %get-tuple-element.17), channel_id=1, replica_groups=mesh['groups'=2,'tensor'=4,'seq'=2,'load'=2] {'tensor'}, dimensions={1}, use_global_device_ids=true | all-gather | bytes 40960 | tf_op jit(solution)/shard_map/all_gather | solution.py:114
  236.8 13.1 %all_gather.25 = bf16[128,128]{0,1:T(8,128)(2,1)S(1)} all-gather(bf16[128,32]{0,1:T(8,128)(2,1)S(1)} %get-tuple-element.18), channel_id=1, replica_groups=mesh['groups'=2,'tensor'=4,'seq'=2,'load'=2] {'tensor'}, dimensions={1}, use_global_device_ids=true | all-gather | bytes 40960 | tf_op jit(solution)/shard_map/all_gather | solution.py:113
  252.7 1.8 collective-permute-start
  254.4 4.6 %convolution_add_fusion = f32[128,4096]{0,1:T(8,128)S(1)} fusion(bf16[128,512]{0,1:T(8,128)(2,1)S(1)} %bitcast.63, bf16[512,4096]{1,0:T(8,128)(2,1)} %all-gather.5.cloned.1.call-done, f32[128,4672]{0,1:T(8,128)} %reduce-scatter.2.cloned.1.call-done), kind=kOutput, calls=%fused_computation.6 | convolution fusion | flops 537395200 | bytes 8519680 | tf_op jit(solution)/shard_map/dot_general | solution.py:16
  259.1 1.7 fusion.42
  262.2 4.9 %fusion.14 = (bf16[128,2048,1]{1,0,2:T(8,128)(2,1)}, bf16[128,2048,1]{1,0,2:T(8,128)(2,1)}) fusion(f32[128,2048,1]{1,0,2:T(8,128)S(1)} %copy.79, f32[128,2048,1]{1,0,2:T(8,128)S(1)} %copy.78, f32[2048]{0:T(1024)S(1)} %fusion.35, f32[128]{0:T(128)S(1)} %subtract_convert_fusion), kind=kLoop, calls=%fused_computation.19 | loop fusion | flops 2359296 | bytes 3154432 | tf_op jit(solution)/shard_map/convert
  267.8 1.6 collective-permute-done.1
  269.4 1.4 collective-permute-start.2
  270.8 1.3 pad_maximum_fusion.1
  272.9 3.5 %collective-permute-done.2 = bf16[128,512]{0,1:T(8,128)(2,1)S(1)} collective-permute-done((bf16[128,512]{0,1:T(8,128)(2,1)}, bf16[128,512]{0,1:T(8,128)(2,1)S(1)}, u32[]{:S(2)}, u32[]{:S(2)}) %collective-permute-start.2) | collective-permute-done | bytes 131104 | tf_op jit(solution)/shard_map/ppermute | solution.py:135
  278.6 5.8 %all_gather.24 = bf16[512,2,128]{2,0,1:T(8,128)(2,1)S(1)} all-gather(bf16[128,2,128]{2,0,1:T(8,128)(2,1)S(1)} %copy.60), channel_id=1, replica_groups=mesh['groups'=2,'tensor'=4,'seq'=2,'load'=2] {'seq','load'}, dimensions={0}, use_global_device_ids=true | all-gather | bytes 327680 | tf_op jit(solution)/shard_map/all_gather | solution.py:155
  284.4 1.3 fusion
  285.7 5.9 %all_gather.27 = bf16[512,2,128]{0,2,1:T(8,128)(2,1)S(1)} all-gather(bf16[128,2,128]{0,2,1:T(8,128)(2,1)S(1)} %bitcast.66), channel_id=1, replica_groups=mesh['groups'=2,'tensor'=4,'seq'=2,'load'=2] {'seq','load'}, dimensions={0}, use_global_device_ids=true | all-gather | bytes 327680 | tf_op jit(solution)/shard_map/all_gather | solution.py:156
  291.6 2.0 fusion.1
  293.7 2.2 fusion.6
  295.9 1.3 copy.67
  (67 shorter events, 13.0 us)
Async XLA Ops:
  8.0 85.9 %copy-start = (bf16[4096,128]{1,0:T(8,128)(2,1)S(1)}, bf16[4096,128]{1,0:T(8,128)(2,1)}, u32[]{:S(2)}) copy-start(bf16[4096,128]{1,0:T(8,128)(2,1)} %param.13) | copy-start | bytes 3145732
  8.0 89.7 %copy-start.4 = (bf16[4096,128]{1,0:T(8,128)(2,1)S(1)}, bf16[4096,128]{1,0:T(8,128)(2,1)}, u32[]{:S(2)}) copy-start(bf16[4096,128]{1,0:T(8,128)(2,1)} %param.14) | copy-start | bytes 3145732
  8.0 85.9 %all-gather.3.cloned.1.call-start = ((), (), s32[]{:S(2)}) async-start(), calls=%async_computation.1 | async-start | bytes 5242880 | tf_op jit(solution)/shard_map/all_gather | solution.py:90
  8.8 214.1 %reduce-scatter.2.cloned.1.call-start = ((), (), s32[]{:S(2)}) async-start(), calls=%async_computation.2 | async-start | bytes 11960320 | tf_op jit(solution)/shard_map/reduce_scatter | solution.py:102
  101.9 26.5 %copy-start.2 = (bf16[512,4096]{1,0:T(8,128)(2,1)S(1)}, bf16[512,4096]{1,0:T(8,128)(2,1)}, u32[]{:S(2)}) copy-start(bf16[512,4096]{1,0:T(8,128)(2,1)} %all-gather.3.cloned.1.call-done) | copy-start | bytes 12582916
  128.4 4.7 %copy-start.3 = (f32[512,4096]{0,1:T(8,128)S(1)}, f32[512,4096]{0,1:T(8,128)}, u32[]{:S(2)}) copy-start(f32[512,4096]{0,1:T(8,128)} %fusion.44) | copy-start | bytes 25165828
  142.9 0.8 copy-start.6
  142.9 0.8 copy-start.7
  142.9 1.0 copy-start.5
  142.9 111.5 %all-gather.5.cloned.1.call-start = ((), (), s32[]{:S(2)}) async-start(), calls=%async_computation.3 | async-start | bytes 6291456 | tf_op jit(solution)/shard_map/all_gather | solution.py:119
  252.7 9.4 %collective-permute-start = (bf16[128,512]{0,1:T(8,128)(2,1)S(1)}, bf16[128,512]{0,1:T(8,128)(2,1)S(1)}, u32[]{:S(2)}, u32[]{:S(2)}) collective-permute-start(bf16[128,512]{0,1:T(8,128)(2,1)S(1)} %select_convert_fusion), channel_id=1, source_target_pairs={{0,4},{4,8},{8,12},{12,0},{1,5},{5,9},{9,13},{13,1},{2,6},{6,10},{... | collective-permute-start | bytes 393224 | tf_op jit(solution)/shard_map/ppermute | solution.py:135
  262.1 7.4 %collective-permute-start.1 = (bf16[128,512]{0,1:T(8,128)(2,1)S(1)}, bf16[128,512]{0,1:T(8,128)(2,1)}, u32[]{:S(2)}, u32[]{:S(2)}) collective-permute-start(bf16[128,512]{0,1:T(8,128)(2,1)S(1)} %collective-permute-done), channel_id=1, source_target_pairs={{0,4},{4,8},{8,12},{12,0},{1,5},{5,9},{9,13},{13,1},{2,6},{6,10},{... | collective-permute-start | bytes 393224 | tf_op jit(solution)/shard_map/ppermute | solution.py:135
  269.4 7.0 %collective-permute-start.2 = (bf16[128,512]{0,1:T(8,128)(2,1)}, bf16[128,512]{0,1:T(8,128)(2,1)S(1)}, u32[]{:S(2)}, u32[]{:S(2)}) collective-permute-start(bf16[128,512]{0,1:T(8,128)(2,1)} %collective-permute-done.1), channel_id=1, source_target_pairs={{0,4},{4,8},{8,12},{12,0},{1,5},{5,9},{9,13},{13,1},{2,6},{6,10},{... | collective-permute-start | bytes 393224 | tf_op jit(solution)/shard_map/ppermute | solution.py:135
  293.7 3.5 %copy-start.1 = (bf16[4096,128]{1,0:T(8,128)(2,1)S(1)}, bf16[4096,128]{1,0:T(8,128)(2,1)}, u32[]{:S(2)}) copy-start(bf16[4096,128]{1,0:T(8,128)(2,1)} %param.13) | copy-start | bytes 3145732
Sparse Core Ops, SparseCore 0:
  10.4 83.4 all-gather.2
  143.0 79.7 reduce-scatter.1
Sparse Core Ops, SparseCore 1:
  144.9 12.6 all-gather.4
